TPU v7x, 512 devices: a whole 4x8x8 slice. The times are simulated.
512 devices in a mesh: tri: 32 (over y, z_lo), vir: 16 (over x, z_hi, core).
Axes of the slice: x: 4, y: 8, z: 8 (z_hi: 2, z_lo: 4; z = z_hi * 4 + z_lo), core: 2. Of those that a mesh axis runs over, the one named last changes fastest.
Arguments:
- amps: bfloat16 [96, 768, 768], P('tri', 'vir'), may hold values from -0.21875 to 0.21875
- vvvo: bfloat16 [96, 768, 128], P('tri', 'vir'), may hold values from -6 to 6
- occ_gap: float32 [64], replicated, may hold values from 0.3 to 1
- vir_gap: float32 [768], P('vir'), may hold values from 0.5 to 2
- pair_gap: float32 [128], replicated, may hold values from 0.5 to 2
- block_sizes: int32 [32], replicated, may hold values from 1 to 3, 64 in all
- roots: int32 [32], replicated, may hold values from 0 to 31, each once
- triples: int32 [384, 2], P('tri'), may hold values from 0 to 31
Outputs:
- density: float32 [768, 128], P('vir')
- grad: float32 [96, 768, 128], P('tri', 'vir')
Inputs may be any that keep to these rules, and one draw needn't show every extreme that they name: `block_sizes`: block sizes sum to 64; at least one block has exactly 3 orbitals. `roots`: each tri index stores exactly one block. `triples`: block numbers; a pair may repeat a block.
All inputs are finite; a program needn't handle non-finite values.
Results may differ from a plain program's by a relative error of at most 0.0003.
Values may be sent and summed in bfloat16 or wider, within the bound.
No kernel may reach another device: no remote copies, remote signals or barrier semaphores. Data moves between devices by JAX's collectives and lax.ppermute only.
A program may use at most 64 MiB of HBM per device.

v0:
```python
import jax
import jax.numpy as jnp
from jax import lax
from jax.sharding import PartitionSpec as P

BMAX = 3


def body(amps, vvvo, occ_gap, vir_gap, pair_gap, block_sizes, roots, triples):
    tri_count = lax.axis_size("tri")
    me = lax.axis_index("tri")
    npair = triples.shape[0]
    nocc = occ_gap.shape[0]
    nrow = tri_count * BMAX
    f32, bf16 = (jnp.float32, jnp.bfloat16)
    slots = jnp.arange(BMAX, dtype=jnp.int32)
    offsets = (jnp.cumsum(block_sizes) - block_sizes).astype(jnp.int32)
    own = roots == me
    own_size = jnp.sum(jnp.where(own, block_sizes, 0))
    own_off = jnp.sum(jnp.where(own, offsets, 0))
    own_gap = occ_gap[jnp.minimum(own_off + slots, nocc - 1)]
    own_live = slots < own_size
    pair_root = roots[triples]
    pair_gap_occ = occ_gap[jnp.minimum(offsets[triples][..., None] + slots, nocc - 1)]
    pair_live = slots < block_sizes[triples][..., None]
    rows = pair_root[..., None] * BMAX + slots
    everything = lax.all_gather(amps, "tri", axis=0, tiled=True)
    table = lax.all_gather(vvvo, "vir", axis=1, tiled=True)
    pick = (rows.reshape(-1)[:, None] == jnp.arange(nrow, dtype=jnp.int32)).astype(bf16)
    picked = jnp.einsum("rb,bad->rad", pick, everything, preferred_element_type=bf16)
    proj = jnp.einsum("rad,kdm->rakm", picked, table, preferred_element_type=f32)
    nv, nk, nm = (proj.shape[1], proj.shape[2], proj.shape[3])
    proj = proj.reshape(npair, 2, BMAX, nv, nk, nm)
    left, right = (proj[:, 0], proj[:, 1])
    base = vir_gap[:, None, None] + own_gap[None, :, None] + pair_gap[None, None, :]
    den = (
        base[None, None, None]
        + pair_gap_occ[:, 0, :, None, None, None, None]
        + pair_gap_occ[:, 1, None, :, None, None, None]
    )
    live = (
        pair_live[:, 0, :, None, None, None, None]
        & pair_live[:, 1, None, :, None, None, None]
        & own_live[None, None, None, None, :, None]
    )
    weighted = jnp.where(live, left[:, :, None] * right[:, None] / den, 0.0)
    dens_part = jnp.sum(weighted * weighted, axis=(0, 1, 2, 4))
    summed = jnp.sum(weighted, axis=2)
    hi_f32 = lax.reduce_precision(summed, exponent_bits=8, mantissa_bits=7)
    hi = hi_f32.astype(bf16)
    lo = (summed - hi_f32).astype(bf16)
    left_rows = picked.reshape(npair, 2, BMAX, nv, -1)[:, 0]
    grad = jnp.einsum("qiad,qiakm->dkm", left_rows, hi, preferred_element_type=f32)
    grad = grad + jnp.einsum("qiad,qiakm->dkm", left_rows, lo, preferred_element_type=f32)
    grad = lax.psum_scatter(grad, "vir", scatter_dimension=0, tiled=True)
    grad = jnp.transpose(grad, (1, 0, 2))
    density = lax.psum(dens_part, "tri") / float(tri_count * npair)
    return (density, grad)


def solution(mesh):
    return jax.shard_map(
        body,
        mesh=mesh,
        in_specs=(
            P("tri", "vir", None),
            P("tri", "vir", None),
            P(),
            P("vir"),
            P(),
            P(),
            P(),
            P("tri", None),
        ),
        out_specs=(P("vir", None), P("tri", "vir", None)),
        check_vma=False,
    )
```

profile of v0, /device:TPU:4, one launch (start us, length us, event | category | flops | bytes accessed | tf_op | source)
XLA Modules:
  0.0 373.6 jit_solution(18367673848902578636)
XLA Ops:
  7.2 0.0 copy-start
  7.2 0.0 copy-start.1
  7.2 0.0 all-gather.2.cloned.1.call-start
  7.2 0.7 all-gather.2.cloned.1.call-update
  7.9 0.0 reduce-scatter.2.cloned.1.call-start
  8.0 0.7 copy.60
  8.7 0.1 reduce-window.9
  8.8 0.1 reduce
  8.9 0.7 compare_select_fusion.1
  9.6 0.1 copy.54
  9.7 0.1 reshape.160
  9.8 0.0 copy-done.1
  9.8 0.0 copy-start.2
  9.8 0.7 gather_fusion
  10.5 0.0 copy-done.2
  10.5 0.7 gather_fusion.1
  11.2 0.6 fusion.17
  11.8 0.7 gather_fusion.3
  12.5 0.1 reshape.183
  12.6 0.1 compare_select_fusion
  12.7 0.1 reshape.192
  12.8 0.0 copy-done
  12.8 0.0 copy-start.5
  12.9 0.0 copy-start.4
  12.9 0.0 copy-start.3
  12.9 1.2 gather_fusion.4
  14.1 0.1 reshape.191
  14.2 0.1 copy.63
  14.3 0.1 copy.64
  14.4 0.1 copy.61
  14.5 0.1 copy.62
  14.6 0.7 fusion.19
  15.3 0.6 gather_fusion.2
  15.9 0.1 reshape.206
  16.0 0.1 iota_add_fusion
  16.1 0.1 add.157
  16.2 0.1 reshape.159
  16.3 0.1 copy.55
  16.4 0.1 copy.57
  16.5 0.1 copy.56
  16.6 0.7 iota_compare_fusion.2
  17.3 0.0 copy-done.5
  17.3 0.1 broadcast_add_fusion.2
  17.4 0.1 broadcast_and_fusion.1
  17.5 0.1 broadcast_and_fusion
  17.6 0.0 copy-done.4
  17.6 0.1 broadcast_add_fusion.1
  17.7 0.0 copy-done.3
  17.7 52.4 %all_gather.7 = bf16[3,768,128]{2,1,0:T(8,128)(2,1)S(1)} all-gather(bf16[3,48,128]{2,1,0:T(8,128)(2,1)S(1)} %copy-done.3), channel_id=1, replica_groups=mesh['tri'=32,'vir'=16] {'vir'}, dimensions={1}, use_global_device_ids=true | all-gather | bytes 626688 | tf_op jit(solution)/shard_map/all_gather | solution.py:28
  70.1 0.2 broadcast_add_fusion
  70.3 124.9 %all-gather.2.cloned.1.call-done = bf16[96,48,768]{2,1,0:T(8,128)(2,1)} async-done(((bf16[3,48,768]{2,1,0:T(8,128)(2,1)}), bf16[96,48,768]{2,1,0:T(8,128)(2,1)}) %all-gather.2.cloned.1.call-update) | async-done | bytes 7077904 | tf_op jit(solution)/shard_map/all_gather | solution.py:27
  195.3 7.9 %fusion = bf16[72,48,768]{2,0,1:T(8,128)(2,1)S(1)} fusion(bf16[96,48,768]{2,1,0:T(8,128)(2,1)} %all-gather.2.cloned.1.call-done, s32[72]{0:T(128)S(1)} %add.157), kind=kOutput, calls=%fused_computation.7 | convolution fusion | flops 509614848 | bytes 12386592 | tf_op jit(solution)/shard_map/rb,bad->rad/dot_general | solution.py:30
  203.2 1.0 copy.65
  204.3 2.9 fusion.3
  207.2 0.5 slice_bitcast_fusion.1
  207.7 3.1 fusion.2
  210.8 0.4 fusion.5
  211.2 1.6 fusion.8
  212.9 2.7 fusion.10
  215.5 0.0 reduce-scatter.2.cloned.1.call-update
  215.5 150.6 %psum.7 = f32[48,128]{1,0:T(8,128)S(1)} all-reduce(f32[48,128]{1,0:T(8,128)S(1)} %get-tuple-element.3), channel_id=1, replica_groups=mesh['tri'=32,'vir'=16] {'tri'}, use_global_device_ids=true, to_apply=%region_4.5 | all-reduce | flops 6144 | bytes 49152 | tf_op jit(solution)/shard_map/psum | solution.py:57
  366.2 0.6 broadcast_multiply_fusion
  366.8 0.0 reduce-scatter.2.cloned.1.call-done
  (7 shorter events, 0.0 us)
Async XLA Ops:
  7.2 5.7 %copy-start = (f32[64]{0:T(128)S(1)}, f32[64]{0:T(128)}, u32[]{:S(2)}) copy-start(f32[64]{0:T(128)} %param.10) | copy-start | bytes 772
  7.2 2.6 copy-start.1
  7.2 188.1 %all-gather.2.cloned.1.call-start = ((), (), s32[]{:S(2)}) async-start(), calls=%async_computation.1 | async-start | bytes 7299072 | tf_op jit(solution)/shard_map/all_gather | solution.py:27
  7.9 358.9 %reduce-scatter.2.cloned.1.call-start = ((), (), s32[]{:S(2)}) async-start(), calls=%async_computation.2 | async-start | bytes 1253376 | tf_op jit(solution)/shard_map/reduce_scatter | solution.py:55
  9.8 0.7 copy-start.2
  12.8 4.5 %copy-start.5 = (f32[48]{0:T(128)S(1)}, f32[48]{0:T(128)}, u32[]{:S(2)}) copy-start(f32[48]{0:T(128)} %param.11) | copy-start | bytes 580
  12.9 4.7 %copy-start.4 = (f32[128]{0:T(128)S(1)}, f32[128]{0:T(128)}, u32[]{:S(2)}) copy-start(f32[128]{0:T(128)} %param.12) | copy-start | bytes 1540
  12.9 4.8 %copy-start.3 = (bf16[3,48,128]{2,1,0:T(8,128)(2,1)S(1)}, bf16[3,48,128]{2,1,0:T(8,128)(2,1)}, u32[]{:S(2)}) copy-start(bf16[3,48,128]{2,1,0:T(8,128)(2,1)} %param.9) | copy-start | bytes 110596
Sparse Core Ops, SparseCore 0:
  10.1 185.1 all-gather.1
  215.7 86.1 reduce-scatter.1
where the time goes:
time: 374 us
  blocking collectives  203 us (54%)
  waiting for transfers between devices  126 us (34%)
  matrix products  15.1 us (4%)
  between operations  14.3 us (4%)
  other arithmetic  7.75 us (2%)
  local copies, waits for them, and re-layouts  7.68 us (2%)
    psum x1, blocking collectives, body(): density = lax.psum(dens_part, 'tri') / float(tri_count * npair)  151 us
    all_gather x1, waiting for transfers between devices, body(): everything = lax.all_gather(amps, 'tri', axis=0, tiled=True)  125 us
    all_gather x1, blocking collectives, body(): table = lax.all_gather(vvvo, 'vir', axis=1, tiled=True)  52.4 us
    dot_general x1, matrix products, body(): jnp.einsum('rb,bad->rad', pick, everything, preferred_element_type=bf16)  7.92 us
  transfers between devices with their start and end apart: 2, of which 1 were waited for; matrix products, arithmetic and copies ran while one was open for 3% of the time, Pallas kernels for 0%

commit v1 on v0

--- a/solution.py
+++ b/solution.py
@@ -7,6 +7,11 @@
 
 
 def body(amps, vvvo, occ_gap, vir_gap, pair_gap, block_sizes, roots, triples):
+
+    def advance_meshes(load, ax_name):
+        low = jnp.sum(lax.all_gather(load, ax_name), 0)
+        return low
+
     tri_count = lax.axis_size("tri")
     me = lax.axis_index("tri")
     npair = triples.shape[0]
@@ -54,7 +59,7 @@
     grad = grad + jnp.einsum("qiad,qiakm->dkm", left_rows, lo, preferred_element_type=f32)
     grad = lax.psum_scatter(grad, "vir", scatter_dimension=0, tiled=True)
     grad = jnp.transpose(grad, (1, 0, 2))
-    density = lax.psum(dens_part, "tri") / float(tri_count * npair)
+    density = advance_meshes(dens_part, "tri") / float(tri_count * npair)
     return (density, grad)
 
 

time: 374 us -> 312 us (0.83)
  the two profiles are of different devices: /device:TPU:4 before, /device:TPU:8 now
where the time goes in v1:
time: 312 us
  waiting for transfers between devices  134 us (43%)
  blocking collectives  133 us (43%)
  matrix products  15.1 us (5%)
  between operations  14.3 us (5%)
  other arithmetic  7.82 us (3%)
  local copies, waits for them, and re-layouts  7.68 us (2%)
    all_gather x1, waiting for transfers between devices, body(): everything = lax.all_gather(amps, 'tri', axis=0, tiled=True)  121 us
    all_gather x1, blocking collectives, advance_meshes(): low = jnp.sum(lax.all_gather(load, ax_name), 0)  77.7 us
    all_gather x1, blocking collectives, body(): table = lax.all_gather(vvvo, 'vir', axis=1, tiled=True)  54.9 us
    reduce_scatter x1, waiting for transfers between devices, body(): grad = lax.psum_scatter(grad, 'vir', scatter_dimension=0, tiled=True)  12.8 us
    dot_general x1, matrix products, body(): jnp.einsum('rb,bad->rad', pick, everything, preferred_element_type=bf16)  7.92 us
  transfers between devices with their start and end apart: 2, of which 2 were waited for; matrix products, arithmetic and copies ran while one was open for 3% of the time, Pallas kernels for 0%

profile of v1, /device:TPU:8, one launch (start us, length us, event | category | flops | bytes accessed | tf_op | source)
XLA Modules:
  0.0 312.1 jit_solution(5299012000034092142)
XLA Ops:
  7.2 0.0 copy-start
  7.2 0.0 copy-start.1
  7.2 0.0 all-gather.3.cloned.1.call-start
  7.2 0.7 all-gather.3.cloned.1.call-update
  7.9 0.0 reduce-scatter.2.cloned.1.call-start
  8.0 0.7 copy.60
  8.7 0.1 reduce-window.9
  8.8 0.1 reduce
  8.9 0.7 compare_select_fusion.1
  9.6 0.1 copy.54
  9.7 0.1 reshape.160
  9.8 0.0 copy-done.1
  9.8 0.0 copy-start.2
  9.8 0.7 gather_fusion
  10.5 0.0 copy-done.2
  10.5 0.7 gather_fusion.1
  11.2 0.6 fusion.17
  11.8 0.7 gather_fusion.3
  12.5 0.1 reshape.183
  12.6 0.1 compare_select_fusion
  12.7 0.1 reshape.192
  12.8 0.0 copy-done
  12.8 0.0 copy-start.5
  12.9 0.0 copy-start.4
  12.9 0.0 copy-start.3
  12.9 1.2 gather_fusion.4
  14.1 0.1 reshape.191
  14.2 0.1 copy.63
  14.3 0.1 copy.64
  14.4 0.1 copy.61
  14.5 0.1 copy.62
  14.6 0.7 fusion.19
  15.3 0.6 gather_fusion.2
  15.9 0.1 reshape.207
  16.0 0.1 iota_add_fusion
  16.1 0.1 add.155
  16.2 0.1 reshape.159
  16.3 0.1 copy.55
  16.4 0.1 copy.57
  16.5 0.1 copy.56
  16.6 0.7 iota_compare_fusion.2
  17.3 0.0 copy-done.5
  17.3 0.1 broadcast_add_fusion.2
  17.4 0.1 broadcast_and_fusion.1
  17.5 0.1 broadcast_and_fusion
  17.6 0.0 copy-done.4
  17.6 0.1 broadcast_add_fusion.1
  17.7 0.0 copy-done.3
  17.7 54.9 %all_gather.13 = bf16[3,768,128]{2,1,0:T(8,128)(2,1)S(1)} all-gather(bf16[3,48,128]{2,1,0:T(8,128)(2,1)S(1)} %copy-done.3), channel_id=1, replica_groups=mesh['tri'=32,'vir'=16] {'vir'}, dimensions={1}, use_global_device_ids=true | all-gather | bytes 626688 | tf_op jit(solution)/shard_map/all_gather | solution.py:33
  72.5 0.2 broadcast_add_fusion
  72.8 121.0 %all-gather.3.cloned.1.call-done = bf16[96,48,768]{2,1,0:T(8,128)(2,1)} async-done(((bf16[3,48,768]{2,1,0:T(8,128)(2,1)}), bf16[96,48,768]{2,1,0:T(8,128)(2,1)}) %all-gather.3.cloned.1.call-update) | async-done | bytes 7077904 | tf_op jit(solution)/shard_map/all_gather | solution.py:32
  193.8 7.9 %fusion = bf16[72,48,768]{2,0,1:T(8,128)(2,1)S(1)} fusion(bf16[96,48,768]{2,1,0:T(8,128)(2,1)} %all-gather.3.cloned.1.call-done, s32[72]{0:T(128)S(1)} %add.155), kind=kOutput, calls=%fused_computation.7 | convolution fusion | flops 509614848 | bytes 12386592 | tf_op jit(solution)/shard_map/rb,bad->rad/dot_general | solution.py:35
  201.7 1.0 copy.65
  202.7 2.9 fusion.3
  205.7 0.5 slice_bitcast_fusion.1
  206.1 3.1 %fusion.2 = (f32[12,3,48,3,128]{4,2,3,1,0:T(8,128)S(1)}, f32[48,128]{1,0:T(8,128)S(1)}) fusion(f32[12,3]{1,0:T(8,128)S(1)} %copy.64, f32[12,3,48,3,128]{4,2,3,1,0:T(8,128)S(1)} %broadcast_add_fusion, f32[12,3,48,3,128]{4,2,3,1,0:T(8,128)S(1)} %get-tuple-element.8, f32[12,3,48,3,128]{4,2,3,1,0:T(8,128)S(1)} %get-tuple-element.7, ...), kind=kLoop, calls=%fused_computation.9 | loop fusion | flops 13264896 | bytes 10641876 | tf_op jit(solution)/shard_map/reduce_sum | solution.py:53
  209.3 0.4 fusion.5
  209.7 1.6 fusion.8
  211.4 2.7 fusion.10
  214.0 0.0 reduce-scatter.2.cloned.1.call-update
  214.0 77.7 %all-gather = f32[1536,128]{1,0:T(8,128)S(1)} all-gather(f32[48,128]{1,0:T(8,128)S(1)} %get-tuple-element.3), channel_id=2, replica_groups=mesh['tri'=32,'vir'=16] {'tri'}, dimensions={0}, use_global_device_ids=true | all-gather | bytes 811008 | tf_op jit(solution)/shard_map/all_gather | solution.py:12
  291.7 0.1 reduce_sum.48
  291.8 0.6 broadcast_multiply_fusion
  292.4 12.8 %reduce-scatter.2.cloned.1.call-done = f32[48,3,128]{2,0,1:T(8,128)} async-done(((f32[768,3,128]{2,0,1:T(8,128)}), f32[48,3,128]{2,0,1:T(8,128)}) %reduce-scatter.2.cloned.1.call-update) | async-done | bytes 73744 | tf_op jit(solution)/shard_map/reduce_scatter | solution.py:60
  (7 shorter events, 0.0 us)
Async XLA Ops:
  7.2 5.7 %copy-start = (f32[64]{0:T(128)S(1)}, f32[64]{0:T(128)}, u32[]{:S(2)}) copy-start(f32[64]{0:T(128)} %param.10) | copy-start | bytes 772
  7.2 2.6 copy-start.1
  7.2 186.6 %all-gather.3.cloned.1.call-start = ((), (), s32[]{:S(2)}) async-start(), calls=%async_computation.1 | async-start | bytes 7299072 | tf_op jit(solution)/shard_map/all_gather | solution.py:32
  7.9 297.3 %reduce-scatter.2.cloned.1.call-start = ((), (), s32[]{:S(2)}) async-start(), calls=%async_computation.2 | async-start | bytes 1253376 | tf_op jit(solution)/shard_map/reduce_scatter | solution.py:60
  9.8 0.7 copy-start.2
  12.8 4.5 %copy-start.5 = (f32[48]{0:T(128)S(1)}, f32[48]{0:T(128)}, u32[]{:S(2)}) copy-start(f32[48]{0:T(128)} %param.11) | copy-start | bytes 580
  12.9 4.7 %copy-start.4 = (f32[128]{0:T(128)S(1)}, f32[128]{0:T(128)}, u32[]{:S(2)}) copy-start(f32[128]{0:T(128)} %param.12) | copy-start | bytes 1540
  12.9 4.8 %copy-start.3 = (bf16[3,48,128]{2,1,0:T(8,128)(2,1)S(1)}, bf16[3,48,128]{2,1,0:T(8,128)(2,1)}, u32[]{:S(2)}) copy-start(bf16[3,48,128]{2,1,0:T(8,128)(2,1)} %param.9) | copy-start | bytes 110596
Sparse Core Ops, SparseCore 0:
  10.1 183.6 all-gather.2
  214.2 91.0 reduce-scatter.1
